TPU v7x, 256 devices: a whole 4x4x8 slice. The times are simulated.
256 devices in a mesh: band: 16 (over y, x), slab: 16 (over z, core).
Axes of the slice: x: 4, y: 4, z: 8, core: 2. Of those that a mesh axis runs over, the one named last changes fastest.
Arguments:
- orbitals: bfloat16 [32, 16777216], P('band', 'slab'), may hold values from -6 to 6
- projectors: bfloat16 [16, 16, 512, 18, 128], P('slab', 'band'), may hold values from -0.5 to 0.5
- piece_block: int32 [16, 16, 512], P('slab', 'band'), may hold values from 0 to 511
- piece_atom: int32 [16, 16, 512], P('slab', 'band'), may hold values from -1 to 1151, as said below
- coupling: float32 [6144, 324], P('slab'), may hold values from -0.6 to 0.6
Outputs:
- applied: bfloat16 [32, 16777216], P('band', 'slab')
Inputs may be any that keep to these rules, and one draw needn't show every extreme that they name: `piece_atom`: each entry is -1 (no atom) or side * 384 + slot with side in 0, 1, 2 and slot < 384: the atom in that slot of the slab side - 1 places away along the slab axis, cyclically. Slabs hold different numbers of atoms and of pieces with an atom.
All inputs are finite; a program needn't handle non-finite values.
Results may differ from a plain program's by a relative error of at most 0.0049.
Values may be sent and summed in bfloat16 or wider, within the bound.
No kernel may reach another device: no remote copies, remote signals or barrier semaphores. Data moves between devices by JAX's collectives and lax.ppermute only.
A program may use at most 128 MiB of HBM per device.

v0:
```python
import jax
import jax.numpy as jnp
from jax import lax
from jax.sharding import PartitionSpec as P

PROJ = 18
BLOCK = 128


def extended(cells, sides, width):
    for axis, dim in sides:
        count = lax.axis_size(axis)
        head = lax.slice_in_dim(cells, 0, width, axis=dim)
        tail = lax.slice_in_dim(cells, cells.shape[dim] - width, cells.shape[dim], axis=dim)
        cells = jnp.concatenate(
            [
                lax.ppermute(tail, axis, [(i, (i + 1) % count) for i in range(count)]),
                cells,
                lax.ppermute(head, axis, [((i + 1) % count, i) for i in range(count)]),
            ],
            axis=dim,
        )
    return cells


def fold_rim(padded):
    return padded[0] + padded[2] + padded[4]


def body(orbitals, projectors, piece_block, piece_atom, coupling):
    slab_waves = lax.all_to_all(orbitals, "band", split_axis=1, concat_axis=0, tiled=True)
    band_count = slab_waves.shape[0]
    blocks = slab_waves.reshape(band_count, -1, BLOCK)
    block_count = blocks.shape[1]
    proj_local = projectors[0, 0]
    index_block = piece_block[0, 0]
    index_atom = piece_atom[0, 0]
    pieces = index_block.shape[0]
    slot_count = coupling.shape[0]
    is_live = index_atom >= 0
    picked = jnp.take(blocks, index_block, axis=1)
    projected = jnp.einsum("pjk,npk->pjn", proj_local, picked, preferred_element_type=jnp.float32)
    target = jnp.where(is_live, index_atom, 3 * slot_count)
    partial_value = jax.ops.segment_sum(
        projected.reshape(pieces, -1), target, num_segments=3 * slot_count + 1
    )
    partial_value = partial_value[: 3 * slot_count].reshape(3, slot_count, -1)
    summed = lax.psum(partial_value, "band")
    summed = fold_rim(extended(summed, (("slab", 0),), 1))[None]
    own_total = summed[0]
    share_rows = own_total.shape[0]
    matrices = coupling.reshape(share_rows, PROJ, PROJ)
    dressed = jnp.einsum(
        "aij,ajn->ain",
        matrices,
        own_total.reshape(share_rows, PROJ, band_count),
        precision=lax.Precision.HIGHEST,
    ).astype(jnp.bfloat16)
    beside_all = extended(dressed[None], (("slab", 0),), 1)
    flat_rows = beside_all.reshape(-1, PROJ, band_count)
    chosen = jnp.take(flat_rows, jnp.where(is_live, index_atom, 0), axis=0)
    chosen = jnp.where(is_live[:, None, None], chosen, jnp.zeros((), jnp.bfloat16))
    spread = jnp.einsum("pjk,pjn->npk", proj_local, chosen, preferred_element_type=jnp.float32)
    result = jnp.zeros((band_count, block_count, BLOCK), jnp.float32).at[:, index_block].add(spread)
    result = result.reshape(band_count, -1).astype(jnp.bfloat16)
    return lax.all_to_all(result, "band", split_axis=0, concat_axis=1, tiled=True)


def solution(mesh):
    placed = (
        P("band", "slab"),
        P("slab", "band", None, None, None),
        P("slab", "band", None),
        P("slab", "band", None),
        P("slab", None),
    )
    return jax.shard_map(
        body, mesh=mesh, in_specs=placed, out_specs=P("band", "slab"), check_vma=False
    )
```

profile of v0, /device:TPU:97, one launch (start us, length us, event | category | flops | bytes accessed | tf_op | source)
XLA Modules:
  0.0 466.2 jit_solution(6507110387990564066)
XLA Ops:
  6.5 6.9 %all-to-all-start = ((bf16[2,16,65536]{2,0,1:T(2,128)(2,1)}), bf16[2,16,65536]{2,0,1:T(2,128)(2,1)}, u32[]{:S(2)}, u32[]{:S(2)}) async-start(bf16[2,16,65536]{2,0,1:T(2,128)(2,1)} %bitcast.41), calls=%async_computation | async-start | bytes 8388608 | tf_op jit(solution)/shard_map/all_to_all | solution.py:31
  13.6 62.3 %all-to-all-done = bf16[2,16,65536]{2,0,1:T(2,128)(2,1)} async-done(((bf16[2,16,65536]{2,0,1:T(2,128)(2,1)}), bf16[2,16,65536]{2,0,1:T(2,128)(2,1)}, u32[]{:S(2)}, u32[]{:S(2)}) %all-to-all-start) | async-done | bytes 4194336 | tf_op jit(solution)/shard_map/all_to_all | solution.py:31
  76.0 11.4 %reshape.116 = bf16[32,512,128]{2,1,0:T(8,128)(2,1)} reshape(bf16[16,2,65536]{2,1,0:T(2,128)(2,1)} %bitcast.7) | data formatting | bytes 8388608 | tf_op jit(solution)/shard_map/reshape | solution.py:33
  87.4 6.8 %copy.103 = bf16[32,512,128]{2,0,1:T(8,128)(2,1)} copy(bf16[32,512,128]{2,1,0:T(8,128)(2,1)} %reshape.116) | data formatting | bytes 8388608 | tf_op jit(solution)/shard_map/reshape | solution.py:33
  94.2 5.4 %gather_fusion = bf16[512,32,128]{2,1,0:T(8,128)(2,1)} fusion(bf16[32,512,128]{2,0,1:T(8,128)(2,1)} %copy.103, s32[1024]{0:T(1024)S(1)} %pad_clamp_fusion.1), kind=kCustom, calls=%fused_computation | custom fusion | bytes 8390656 | tf_op jit(solution)/shard_map/jit(_take)/gather | solution.py:41
  99.6 10.9 %fusion.11 = f32[512,18,32]{2,1,0:T(8,128)} fusion(bf16[512,18,128]{2,0,1:T(8,128)(2,1)S(1)} %bitcast.35, bf16[512,32,128]{2,1,0:T(8,128)(2,1)} %gather_fusion, pred[512]{0:T(512)(128)(4,1)S(1)} %compare_and_fusion), kind=kOutput, calls=%fused_computation.16 | convolution fusion | flops 77594624 | bytes 7733760 | tf_op jit(solution)/shard_map/pjk,npk->pjn/dot_general | solution.py:42
  110.5 4.5 copy.105
  116.5 6.4 %scatter_custom_fusion = f32[1153,576]{1,0:T(8,128)} fusion(s32[512]{0:T(512)S(1)} %bitcast.48, f32[512,576]{1,0:T(8,128)} %copy.106, f32[]{:T(128)} %constant.12.clone.1), kind=kCustom, calls=%fused_computation.21 | custom fusion | flops 294912 | bytes 2657024 | tf_op jit(solution)/shard_map/scatter-add | solution.py:44
  126.5 4.6 copy.107
  131.1 103.1 %all-reduce.2.cloned.1.call-done = f32[3,384,576]{1,2,0:T(8,128)} async-done(((f32[3,384,576]{1,2,0:T(8,128)}), f32[3,384,576]{1,2,0:T(8,128)}) %all-reduce.2.cloned.1.call-update) | async-done | bytes 2654224 | tf_op jit(solution)/shard_map/psum | solution.py:48
  244.0 6.9 %collective-permute-done = f32[1,384,576]{1,2,0:T(8,128)} collective-permute-done((f32[1,384,576]{1,2,0:T(8,128)}, f32[1,384,576]{1,2,0:T(8,128)}, u32[]{:S(2)}, u32[]{:S(2)}) %collective-permute-start) | collective-permute-done | bytes 884768 | tf_op jit(solution)/shard_map/ppermute | solution.py:17
  250.9 3.7 collective-permute-done.1
  259.8 11.2 %convert_bitcast_fusion = bf16[1,384,18,32]{3,2,1,0:T(8,128)(2,1)} fusion(f32[384,18,32]{2,1,0:T(8,128)} %copy.108, f32[384,18,18]{2,1,0:T(8,128)} %copy.109), kind=kOutput, calls=%fused_computation.17 | convolution fusion | flops 47996928 | bytes 1824768 | tf_op jit(solution)/shard_map/aij,ajn->ain/dot_general | solution.py:53
  274.4 4.7 %collective-permute-done.2 = bf16[1,384,18,32]{1,3,2,0:T(8,128)(2,1)} collective-permute-done((bf16[1,384,18,32]{1,3,2,0:T(8,128)(2,1)S(1)}, bf16[1,384,18,32]{1,3,2,0:T(8,128)(2,1)}, u32[]{:S(2)}, u32[]{:S(2)}) %collective-permute-start.2) | collective-permute-done | bytes 442400 | tf_op jit(solution)/shard_map/ppermute | solution.py:17
  279.2 3.6 copy.112
  285.4 6.9 %pad_maximum_fusion = bf16[3,384,18,32]{3,2,1,0:T(8,128)(2,1)} fusion(bf16[1,384,18,32]{3,2,1,0:T(8,128)(2,1)} %copy.113, bf16[1,384,18,32]{3,2,1,0:T(8,128)(2,1)} %convert_bitcast_fusion, bf16[1,384,18,32]{3,2,1,0:T(8,128)(2,1)} %copy.112), kind=kLoop, calls=%fused_computation.4 | loop fusion | flops 1327104 | bytes 2654208 | tf_op jit(solution)/shard_map/concatenate | solution.py:15
  292.3 6.0 %gather_fusion.1 = bf16[512,18,32]{2,1,0:T(8,128)(2,1)} fusion(bf16[1152,18,32]{2,1,0:T(8,128)(2,1)} %bitcast.38, s32[1024]{0:T(1024)S(1)} %pad_clamp_fusion), kind=kCustom, calls=%fused_computation.1 | custom fusion | bytes 1181696 | tf_op jit(solution)/shard_map/jit(_take)/gather | solution.py:61
  298.2 13.1 %fusion.4 = f32[512,32,128]{2,1,0:T(8,128)} fusion(bf16[512,18,128]{2,0,1:T(8,128)(2,1)S(1)} %bitcast.36, bf16[512,18,32]{2,1,0:T(8,128)(2,1)} %gather_fusion.1, pred[512]{0:T(512)(128)(4,1)S(1)} %get-tuple-element.8, pred[512]{0:T(512)(128)(4,1)S(1)} %get-tuple-element.7), kind=kOutput, calls=%fused_computation.9 | convolution fusion | flops 76087296 | bytes 11338752 | tf_op jit(solution)/shard_map/pjk,pjn->npk/dot_general | solution.py:63
  311.3 4.3 broadcast_in_dim.47
  315.6 67.5 %scatter_fusion = f32[32,512,128]{2,0,1:T(8,128)} fusion(f32[32,512,128]{2,0,1:T(8,128)} %broadcast_in_dim.47, s32[512]{0:T(512)S(1)} %bitcast.44, f32[512,32,128]{2,1,0:T(8,128)} %fusion.4), kind=kCustom, calls=%fused_computation.3 | custom fusion | flops 2097152 | bytes 25167872 | tf_op jit(solution)/shard_map/scatter-add | solution.py:64
  383.1 4.4 convert_element_type.15
  387.5 3.6 copy.117
  391.1 10.4 %convert_element_type.16 = bf16[16,2,65536]{2,1,0:T(2,128)(2,1)} reshape(bf16[32,512,128]{2,1,0:T(8,128)(2,1)} %copy.117) | data formatting | bytes 8388608 | tf_op jit(solution)/shard_map/convert_element_type | solution.py:65
  401.5 55.9 %all_to_all.32 = bf16[16,2,65536]{2,1,0:T(2,128)(2,1)S(1)} all-to-all(bf16[16,2,65536]{2,1,0:T(2,128)(2,1)} %convert_element_type.16), channel_id=1, replica_groups=mesh['band'=16,'slab'=16] {'band'}, dimensions={0} | all-to-all | bytes 8388608 | tf_op jit(solution)/shard_map/all_to_all | solution.py:66
  (31 shorter events, 28.3 us)
Async XLA Ops:
  6.5 93.1 %copy-start = (bf16[1,1,512,18,128]{4,2,3,1,0:T(8,128)(2,1)S(1)}, bf16[1,1,512,18,128]{4,2,3,1,0:T(8,128)(2,1)}, u32[]{:S(2)}) copy-start(bf16[1,1,512,18,128]{4,2,3,1,0:T(8,128)(2,1)} %param.6) | copy-start | bytes 7077892
  6.5 7.0 %copy-start.3 = (s32[1,1,512]{2,1,0:T(1,128)S(1)}, s32[1,1,512]{2,1,0:T(1,128)}, u32[]{:S(2)}) copy-start(s32[1,1,512]{2,1,0:T(1,128)} %param.7) | copy-start | bytes 6148
  6.5 7.0 %copy-start.2 = (s32[1,1,512]{2,1,0:T(1,128)S(1)}, s32[1,1,512]{2,1,0:T(1,128)}, u32[]{:S(2)}) copy-start(s32[1,1,512]{2,1,0:T(1,128)} %param.8) | copy-start | bytes 6148
  6.5 69.4 %all-to-all-start = ((bf16[2,16,65536]{2,0,1:T(2,128)(2,1)}), bf16[2,16,65536]{2,0,1:T(2,128)(2,1)}, u32[]{:S(2)}, u32[]{:S(2)}) async-start(bf16[2,16,65536]{2,0,1:T(2,128)(2,1)} %bitcast.41), calls=%async_computation | async-start | bytes 8388608 | tf_op jit(solution)/shard_map/all_to_all | solution.py:31
  13.5 220.7 %all-reduce.2.cloned.1.call-start = ((), (), s32[]{:S(2)}) async-start(), calls=%async_computation.2 | async-start | bytes 5308416 | tf_op jit(solution)/shard_map/psum | solution.py:48
  131.0 109.5 %copy-start.1 = (f32[384,324]{0,1:T(8,128)S(1)}, f32[384,324]{0,1:T(8,128)}, u32[]{:S(2)}) copy-start(f32[384,324]{0,1:T(8,128)} %param.9) | copy-start | bytes 1492996
  236.9 13.9 %collective-permute-start = (f32[1,384,576]{1,2,0:T(8,128)}, f32[1,384,576]{1,2,0:T(8,128)}, u32[]{:S(2)}, u32[]{:S(2)}) collective-permute-start(f32[1,384,576]{1,2,0:T(8,128)} %get-tuple-element.5), channel_id=1, source_target_pairs={{0,1},{1,2},{2,3},{3,4},{4,5},{5,6},{6,7},{7,8},{8,9},{9,10},{10,1... | collective-permute-start | bytes 2654216 | tf_op jit(solution)/shard_map/ppermute | solution.py:17
  240.5 14.0 %collective-permute-start.1 = (f32[1,384,576]{1,2,0:T(8,128)}, f32[1,384,576]{1,2,0:T(8,128)}, u32[]{:S(2)}, u32[]{:S(2)}) collective-permute-start(f32[1,384,576]{1,2,0:T(8,128)} %get-tuple-element.6), channel_id=1, source_target_pairs={{1,0},{2,1},{3,2},{4,3},{5,4},{6,5},{7,6},{8,7},{9,8},{10,9},{11,1... | collective-permute-start | bytes 2654216 | tf_op jit(solution)/shard_map/ppermute | solution.py:19
  273.9 5.3 %collective-permute-start.2 = (bf16[1,384,18,32]{1,3,2,0:T(8,128)(2,1)S(1)}, bf16[1,384,18,32]{1,3,2,0:T(8,128)(2,1)}, u32[]{:S(2)}, u32[]{:S(2)}) collective-permute-start(bf16[1,384,18,32]{1,3,2,0:T(8,128)(2,1)S(1)} %copy.110), channel_id=1, source_target_pairs={{0,1},{1,2},{2,3},{3,4},{4,5},{5,6},{6,7},{7,8},{8,9},{9,10},{10,1... | collective-permute-start | bytes 1327112 | tf_op jit(solution)/shard_map/ppermute | solution.py:17
  273.9 9.0 %collective-permute-start.3 = (bf16[1,384,18,32]{1,3,2,0:T(8,128)(2,1)S(1)}, bf16[1,384,18,32]{1,3,2,0:T(8,128)(2,1)S(1)}, u32[]{:S(2)}, u32[]{:S(2)}) collective-permute-start(bf16[1,384,18,32]{1,3,2,0:T(8,128)(2,1)S(1)} %copy.110), channel_id=1, source_target_pairs={{1,0},{2,1},{3,2},{4,3},{5,4},{6,5},{7,6},{8,7},{9,8},{10,9},{11,1... | collective-permute-start | bytes 1327112 | tf_op jit(solution)/shard_map/ppermute | solution.py:19
Sparse Core Ops, SparseCore 0:
  131.2 102.9 all-reduce.1
where the time goes:
time: 468 us; the launch traced here: 466 us
  waiting for transfers between devices  181 us (39%)
  other arithmetic  87 us (19%)
  local copies, waits for them, and re-layouts  82.8 us (18%)
  blocking collectives  55.9 us (12%)
  matrix products  35.1 us (8%)
  between operations  13.5 us (3%)
  starting transfers between devices  11.1 us (2%)
    psum x1, waiting for transfers between devices, body(): summed = lax.psum(partial_value, 'band')  103 us
    scatter-add x1, other arithmetic, body(): jnp.zeros((band_count, block_count, BLOCK), jnp.float32).at[:, index_block]  67.5 us
    all_to_all x1, waiting for transfers between devices, body(): lax.all_to_all(orbitals, 'band', split_axis=1, concat_axis=0, tiled=True)  62.3 us
    all_to_all x1, blocking collectives, body(): lax.all_to_all(result, 'band', split_axis=0, concat_axis=1, tiled=True)  55.9 us
    reshape x2, local copies, waits for them, and re-layouts, body(): blocks = slab_waves.reshape(band_count, -1, BLOCK)  18.2 us
    convert_element_type x2, local copies, waits for them, and re-layouts, body(): result = result.reshape(band_count, -1).astype(jnp.bfloat16)  14 us
    dot_general x1, matrix products, body(): jnp.einsum('pjk,pjn->npk', proj_local, chosen, preferred_element_type=jnp...  13.1 us
    ppermute x2, waiting for transfers between devices, extended(): lax.ppermute(tail, axis, [(i, (i + 1) % count) for i in range(count)])  11.6 us
  transfers between devices with their start and end apart: 6, of which 6 were waited for; matrix products, arithmetic and copies ran while one was open for 2% of the time, Pallas kernels for 0%

commit v1 on v0

--- a/solution.py
+++ b/solution.py
@@ -45,7 +45,13 @@
         projected.reshape(pieces, -1), target, num_segments=3 * slot_count + 1
     )
     partial_value = partial_value[: 3 * slot_count].reshape(3, slot_count, -1)
-    summed = lax.psum(partial_value, "band")
+    n_axis = lax.axis_size("band")
+    summed = partial_value
+    for j0 in [
+        [(pp, pp ^ dev_i) for pp in range(n_axis)] for dev_i in (1, 2, 4, 8, 16) if dev_i < n_axis
+    ]:
+        arr_now = lax.ppermute(summed, "band", j0)
+        summed = summed + arr_now
     summed = fold_rim(extended(summed, (("slab", 0),), 1))[None]
     own_total = summed[0]
     share_rows = own_total.shape[0]

time: 468 us -> 587 us (1.25)
  waiting for transfers between devices: 181 us -> 304 us
  between operations: 13.5 us -> 0.14 us
  starting transfers between devices: 11.1 us -> 17.4 us
    ppermute x0 -> x4, waiting for transfers between devices: none -> 226 us  [body(): arr_now = lax.ppermute(summed, 'band', j0)]
    psum x1 -> x0, waiting for transfers between devices: 103 us -> none  [body(): summed = lax.psum(partial_value, 'band')]
  transfers between devices with their start and end apart: 6 -> 9, of which waited for: 6 -> 9; matrix products, arithmetic and copies ran while one was open for 2% -> 1% of each run, Pallas kernels for 0% -> 0%
where the time goes in v1:
time: 587 us; the launch traced here: 585 us
  waiting for transfers between devices  304 us (52%)
  other arithmetic  89.8 us (15%)
  local copies, waits for them, and re-layouts  83.2 us (14%)
  blocking collectives  55.1 us (9%)
  matrix products  35.1 us (6%)
  starting transfers between devices  17.4 us (3%)
    ppermute x4, waiting for transfers between devices, body(): arr_now = lax.ppermute(summed, 'band', j0)  226 us
    scatter-add x1, other arithmetic, body(): jnp.zeros((band_count, block_count, BLOCK), jnp.float32).at[:, index_block]  67.3 us
    all_to_all x1, waiting for transfers between devices, body(): lax.all_to_all(orbitals, 'band', split_axis=1, concat_axis=0, tiled=True)  62.4 us
    all_to_all x1, blocking collectives, body(): lax.all_to_all(result, 'band', split_axis=0, concat_axis=1, tiled=True)  55.1 us
    reshape x2, local copies, waits for them, and re-layouts, body(): blocks = slab_waves.reshape(band_count, -1, BLOCK)  18.2 us
    convert_element_type x2, local copies, waits for them, and re-layouts, body(): result = result.reshape(band_count, -1).astype(jnp.bfloat16)  14.1 us
    dot_general x1, matrix products, body(): jnp.einsum('pjk,pjn->npk', proj_local, chosen, preferred_element_type=jnp...  13 us
  transfers between devices with their start and end apart: 9, of which 9 were waited for; matrix products, arithmetic and copies ran while one was open for 1% of the time, Pallas kernels for 0%

profile of v1, /device:TPU:97, one launch (start us, length us, event | category | flops | bytes accessed | tf_op | source)
XLA Modules:
  0.0 584.7 jit_solution(15468078543818034140)
XLA Ops:
  0.0 6.9 %all-to-all-start = ((bf16[2,16,65536]{2,0,1:T(2,128)(2,1)}), bf16[2,16,65536]{2,0,1:T(2,128)(2,1)}, u32[]{:S(2)}, u32[]{:S(2)}) async-start(bf16[2,16,65536]{2,0,1:T(2,128)(2,1)} %bitcast.41), calls=%async_computation | async-start | bytes 8388608 | tf_op jit(solution)/shard_map/all_to_all | solution.py:31
  7.0 62.4 %all-to-all-done = bf16[2,16,65536]{2,0,1:T(2,128)(2,1)} async-done(((bf16[2,16,65536]{2,0,1:T(2,128)(2,1)}), bf16[2,16,65536]{2,0,1:T(2,128)(2,1)}, u32[]{:S(2)}, u32[]{:S(2)}) %all-to-all-start) | async-done | bytes 4194336 | tf_op jit(solution)/shard_map/all_to_all | solution.py:31
  69.4 11.4 %reshape.116 = bf16[32,512,128]{2,1,0:T(8,128)(2,1)} reshape(bf16[16,2,65536]{2,1,0:T(2,128)(2,1)} %bitcast.7) | data formatting | bytes 8388608 | tf_op jit(solution)/shard_map/reshape | solution.py:33
  80.8 6.8 %copy.135 = bf16[32,512,128]{2,0,1:T(8,128)(2,1)} copy(bf16[32,512,128]{2,1,0:T(8,128)(2,1)} %reshape.116) | data formatting | bytes 8388608 | tf_op jit(solution)/shard_map/reshape | solution.py:33
  87.7 5.4 gather_fusion
  93.1 10.9 %fusion.11 = f32[512,18,32]{2,1,0:T(8,128)} fusion(bf16[512,18,128]{2,0,1:T(8,128)(2,1)S(1)} %bitcast.35, bf16[512,32,128]{2,1,0:T(8,128)(2,1)} %gather_fusion, pred[512]{0:T(512)(128)(4,1)S(1)} %compare_and_fusion), kind=kOutput, calls=%fused_computation.16 | convolution fusion | flops 77594624 | bytes 7733760 | tf_op jit(solution)/shard_map/pjk,npk->pjn/dot_general | solution.py:42
  104.0 4.5 copy.137
  110.0 6.5 %scatter_custom_fusion = f32[1153,576]{1,0:T(8,128)} fusion(s32[512]{0:T(512)S(1)} %bitcast.48, f32[512,576]{1,0:T(8,128)} %copy.138, f32[]{:T(128)} %constant.12.clone.1), kind=kCustom, calls=%fused_computation.21 | custom fusion | flops 294912 | bytes 2657024 | tf_op jit(solution)/shard_map/scatter-add | solution.py:44
  120.1 4.6 copy.140
  124.7 57.6 %collective-permute-done = f32[3,384,576]{1,2,0:T(8,128)S(1)} collective-permute-done((f32[3,384,576]{1,2,0:T(8,128)}, f32[3,384,576]{1,2,0:T(8,128)S(1)}, u32[]{:S(2)}, u32[]{:S(2)}) %collective-permute-start) | collective-permute-done | bytes 2654240 | tf_op jit(solution)/shard_map/ppermute | solution.py:53
  185.0 57.4 %collective-permute-done.1 = f32[3,384,576]{1,2,0:T(8,128)S(1)} collective-permute-done((f32[3,384,576]{1,2,0:T(8,128)S(1)}, f32[3,384,576]{1,2,0:T(8,128)S(1)}, u32[]{:S(2)}, u32[]{:S(2)}) %collective-permute-start.1) | collective-permute-done | bytes 2654240 | tf_op jit(solution)/shard_map/ppermute | solution.py:53
  242.8 55.6 %collective-permute-done.2 = f32[3,384,576]{1,2,0:T(8,128)S(1)} collective-permute-done((f32[3,384,576]{1,2,0:T(8,128)S(1)}, f32[3,384,576]{1,2,0:T(8,128)S(1)}, u32[]{:S(2)}, u32[]{:S(2)}) %collective-permute-start.2) | collective-permute-done | bytes 2654240 | tf_op jit(solution)/shard_map/ppermute | solution.py:53
  300.3 55.9 %collective-permute-done.3 = f32[3,384,576]{1,2,0:T(8,128)S(1)} collective-permute-done((f32[3,384,576]{1,2,0:T(8,128)S(1)}, f32[3,384,576]{1,2,0:T(8,128)S(1)}, u32[]{:S(2)}, u32[]{:S(2)}) %collective-permute-start.3) | collective-permute-done | bytes 2654240 | tf_op jit(solution)/shard_map/ppermute | solution.py:53
  359.4 7.4 %collective-permute-start.4 = (f32[1,384,576]{1,2,0:T(8,128)}, f32[1,384,576]{1,2,0:T(8,128)}, u32[]{:S(2)}, u32[]{:S(2)}) collective-permute-start(f32[1,384,576]{1,2,0:T(8,128)} %get-tuple-element.5), channel_id=1, source_target_pairs={{0,1},{1,2},{2,3},{3,4},{4,5},{5,6},{6,7},{7,8},{8,9},{9,10},{10,1... | collective-permute-start | bytes 2654216 | tf_op jit(solution)/shard_map/ppermute | solution.py:17
  370.5 6.7 %collective-permute-done.4 = f32[1,384,576]{1,2,0:T(8,128)} collective-permute-done((f32[1,384,576]{1,2,0:T(8,128)}, f32[1,384,576]{1,2,0:T(8,128)}, u32[]{:S(2)}, u32[]{:S(2)}) %collective-permute-start.4) | collective-permute-done | bytes 884768 | tf_op jit(solution)/shard_map/ppermute | solution.py:17
  386.0 11.2 %convert_bitcast_fusion = bf16[1,384,18,32]{3,2,1,0:T(8,128)(2,1)} fusion(f32[384,18,32]{2,1,0:T(8,128)} %copy.141, f32[384,18,18]{2,1,0:T(8,128)} %copy.142), kind=kOutput, calls=%fused_computation.17 | convolution fusion | flops 47996928 | bytes 1824768 | tf_op jit(solution)/shard_map/aij,ajn->ain/dot_general | solution.py:59
  400.7 4.7 collective-permute-done.6
  411.7 6.9 %pad_maximum_fusion = bf16[3,384,18,32]{3,2,1,0:T(8,128)(2,1)} fusion(bf16[1,384,18,32]{3,2,1,0:T(8,128)(2,1)} %copy.146, bf16[1,384,18,32]{3,2,1,0:T(8,128)(2,1)} %convert_bitcast_fusion, bf16[1,384,18,32]{3,2,1,0:T(8,128)(2,1)} %copy.145), kind=kLoop, calls=%fused_computation.4 | loop fusion | flops 1327104 | bytes 2654208 | tf_op jit(solution)/shard_map/concatenate | solution.py:15
  418.5 6.0 %gather_fusion.1 = bf16[512,18,32]{2,1,0:T(8,128)(2,1)} fusion(bf16[1152,18,32]{2,1,0:T(8,128)(2,1)} %bitcast.38, s32[1024]{0:T(1024)S(1)} %pad_clamp_fusion), kind=kCustom, calls=%fused_computation.1 | custom fusion | bytes 1181696 | tf_op jit(solution)/shard_map/jit(_take)/gather | solution.py:67
  424.5 13.0 %fusion.4 = f32[512,32,128]{2,1,0:T(8,128)} fusion(bf16[512,18,128]{2,0,1:T(8,128)(2,1)S(1)} %bitcast.36, bf16[512,18,32]{2,1,0:T(8,128)(2,1)} %gather_fusion.1, pred[512]{0:T(512)(128)(4,1)S(1)} %get-tuple-element.8, pred[512]{0:T(512)(128)(4,1)S(1)} %get-tuple-element.7), kind=kOutput, calls=%fused_computation.9 | convolution fusion | flops 76087296 | bytes 11338752 | tf_op jit(solution)/shard_map/pjk,pjn->npk/dot_general | solution.py:69
  441.8 67.3 %scatter_fusion = f32[32,512,128]{2,0,1:T(8,128)} fusion(f32[32,512,128]{2,0,1:T(8,128)} %broadcast_in_dim.47, s32[512]{0:T(512)S(1)} %bitcast.44, f32[512,32,128]{2,1,0:T(8,128)} %fusion.4), kind=kCustom, calls=%fused_computation.3 | custom fusion | flops 2097152 | bytes 25167872 | tf_op jit(solution)/shard_map/scatter-add | solution.py:70
  509.1 4.4 convert_element_type.15
  517.2 10.5 %convert_element_type.16 = bf16[16,2,65536]{2,1,0:T(2,128)(2,1)} reshape(bf16[32,512,128]{2,1,0:T(8,128)(2,1)} %copy.150) | data formatting | bytes 8388608 | tf_op jit(solution)/shard_map/convert_element_type | solution.py:71
  527.6 55.1 %all_to_all.32 = bf16[16,2,65536]{2,1,0:T(2,128)(2,1)S(1)} all-to-all(bf16[16,2,65536]{2,1,0:T(2,128)(2,1)} %convert_element_type.16), channel_id=1, replica_groups=mesh['band'=16,'slab'=16] {'band'}, dimensions={0} | all-to-all | bytes 8388608 | tf_op jit(solution)/shard_map/all_to_all | solution.py:72
  (42 shorter events, 45.6 us)
Async XLA Ops:
  0.0 93.1 %copy-start = (bf16[1,1,512,18,128]{4,2,3,1,0:T(8,128)(2,1)S(1)}, bf16[1,1,512,18,128]{4,2,3,1,0:T(8,128)(2,1)}, u32[]{:S(2)}) copy-start(bf16[1,1,512,18,128]{4,2,3,1,0:T(8,128)(2,1)} %param.6) | copy-start | bytes 7077892
  0.0 7.0 %copy-start.4 = (s32[1,1,512]{2,1,0:T(1,128)S(1)}, s32[1,1,512]{2,1,0:T(1,128)}, u32[]{:S(2)}) copy-start(s32[1,1,512]{2,1,0:T(1,128)} %param.7) | copy-start | bytes 6148
  0.0 7.0 %copy-start.3 = (s32[1,1,512]{2,1,0:T(1,128)S(1)}, s32[1,1,512]{2,1,0:T(1,128)}, u32[]{:S(2)}) copy-start(s32[1,1,512]{2,1,0:T(1,128)} %param.8) | copy-start | bytes 6148
  0.0 69.4 %all-to-all-start = ((bf16[2,16,65536]{2,0,1:T(2,128)(2,1)}), bf16[2,16,65536]{2,0,1:T(2,128)(2,1)}, u32[]{:S(2)}, u32[]{:S(2)}) async-start(bf16[2,16,65536]{2,0,1:T(2,128)(2,1)} %bitcast.41), calls=%async_computation | async-start | bytes 8388608 | tf_op jit(solution)/shard_map/all_to_all | solution.py:31
  124.7 57.6 %collective-permute-start = (f32[3,384,576]{1,2,0:T(8,128)}, f32[3,384,576]{1,2,0:T(8,128)S(1)}, u32[]{:S(2)}, u32[]{:S(2)}) collective-permute-start(f32[3,384,576]{1,2,0:T(8,128)} %copy.140), channel_id=1, source_target_pairs={{0,16},{16,0},{32,48},{48,32},{64,80},{80,64},{96,112},{112,96},{1... | collective-permute-start | bytes 7962632 | tf_op jit(solution)/shard_map/ppermute | solution.py:53
  184.3 58.1 %collective-permute-start.1 = (f32[3,384,576]{1,2,0:T(8,128)S(1)}, f32[3,384,576]{1,2,0:T(8,128)S(1)}, u32[]{:S(2)}, u32[]{:S(2)}) collective-permute-start(f32[3,384,576]{1,2,0:T(8,128)S(1)} %add.79), channel_id=1, source_target_pairs={{0,32},{16,48},{32,0},{48,16},{64,96},{80,112},{96,64},{112,80},{1... | collective-permute-start | bytes 7962632 | tf_op jit(solution)/shard_map/ppermute | solution.py:53
  242.7 55.7 %collective-permute-start.2 = (f32[3,384,576]{1,2,0:T(8,128)S(1)}, f32[3,384,576]{1,2,0:T(8,128)S(1)}, u32[]{:S(2)}, u32[]{:S(2)}) collective-permute-start(f32[3,384,576]{1,2,0:T(8,128)S(1)} %add.80), channel_id=1, source_target_pairs={{0,64},{16,80},{32,96},{48,112},{64,0},{80,16},{96,32},{112,48},{1... | collective-permute-start | bytes 7962632 | tf_op jit(solution)/shard_map/ppermute | solution.py:53
  298.6 57.6 %collective-permute-start.3 = (f32[3,384,576]{1,2,0:T(8,128)S(1)}, f32[3,384,576]{1,2,0:T(8,128)S(1)}, u32[]{:S(2)}, u32[]{:S(2)}) collective-permute-start(f32[3,384,576]{1,2,0:T(8,128)S(1)} %add.81), channel_id=1, source_target_pairs={{0,128},{16,144},{32,160},{48,176},{64,192},{80,208},{96,224},{112... | collective-permute-start | bytes 7962632 | tf_op jit(solution)/shard_map/ppermute | solution.py:53
  356.5 1.5 copy-start.1
  358.0 8.8 %copy-start.2 = (f32[384,324]{0,1:T(8,128)S(1)}, f32[384,324]{0,1:T(8,128)}, u32[]{:S(2)}) copy-start(f32[384,324]{0,1:T(8,128)} %param.9) | copy-start | bytes 1492996
  359.4 17.7 %collective-permute-start.4 = (f32[1,384,576]{1,2,0:T(8,128)}, f32[1,384,576]{1,2,0:T(8,128)}, u32[]{:S(2)}, u32[]{:S(2)}) collective-permute-start(f32[1,384,576]{1,2,0:T(8,128)} %get-tuple-element.5), channel_id=1, source_target_pairs={{0,1},{1,2},{2,3},{3,4},{4,5},{5,6},{6,7},{7,8},{8,9},{9,10},{10,1... | collective-permute-start | bytes 2654216 | tf_op jit(solution)/shard_map/ppermute | solution.py:17
  366.8 14.0 %collective-permute-start.5 = (f32[1,384,576]{1,2,0:T(8,128)}, f32[1,384,576]{1,2,0:T(8,128)}, u32[]{:S(2)}, u32[]{:S(2)}) collective-permute-start(f32[1,384,576]{1,2,0:T(8,128)} %get-tuple-element.6), channel_id=1, source_target_pairs={{1,0},{2,1},{3,2},{4,3},{5,4},{6,5},{7,6},{8,7},{9,8},{10,9},{11,1... | collective-permute-start | bytes 2654216 | tf_op jit(solution)/shard_map/ppermute | solution.py:19
  400.1 5.3 collective-permute-start.6
  400.2 9.0 %collective-permute-start.7 = (bf16[1,384,18,32]{1,3,2,0:T(8,128)(2,1)S(1)}, bf16[1,384,18,32]{1,3,2,0:T(8,128)(2,1)S(1)}, u32[]{:S(2)}, u32[]{:S(2)}) collective-permute-start(bf16[1,384,18,32]{1,3,2,0:T(8,128)(2,1)S(1)} %copy.143), channel_id=1, source_target_pairs={{1,0},{2,1},{3,2},{4,3},{5,4},{6,5},{7,6},{8,7},{9,8},{10,9},{11,1... | collective-permute-start | bytes 1327112 | tf_op jit(solution)/shard_map/ppermute | solution.py:19
